TPU v7x, 32 devices: a whole 2x2x4 slice. The times are simulated.
32 devices in a mesh: groups: 2 (over y), ctx: 4 (over z), head: 4 (over x, core).
Axes of the slice: x: 2, y: 2, z: 4, core: 2. Of those that a mesh axis runs over, the one named last changes fastest.
Arguments:
- hidden_in: bfloat16 [2048, 4096], P(('groups', 'ctx'), 'head'), parts along dimension 0, may hold values from -6 to 6
- norm_gain: bfloat16 [4096], P('head'), may hold values from 0.099609375 to 1.8984375
- w_query: bfloat16 [4096, 2048], P('ctx', 'head'), may hold values from -8 to 8
- w_key: bfloat16 [4096, 512], P('ctx', 'head'), may hold values from -8 to 8
- w_value: bfloat16 [4096, 512], P('ctx', 'head'), may hold values from -0.09375 to 0.09375
- w_out: bfloat16 [2048, 4096], P('head', 'ctx'), may hold values from -3 to 3
- session_ids: int32 [2048], P('groups'), parts along dimension 0, may hold values from 0 to 3, never falling along the last dimension, each value on 1 to 512 neighbouring positions
- block_anchor: int32 [16], P('groups'), parts along dimension 0, may hold values from 0 to 7, each once
Outputs:
- block_update: bfloat16 [2048, 4096], P(('groups', 'ctx'), 'head'), parts along dimension 0
There are 2 independent parts, one for each index of `groups`. A program takes and returns all parts, laid end to end along the dimension named above; an argument that names none is the same for every part. Nothing has to cross between parts.
Inputs may be any that keep to these rules, and one draw needn't show every extreme that they name: `session_ids`: session numbers never fall along the contiguous order; 4 sessions, each of 1 to 512 tokens, one of exactly 512. `block_anchor`: each of the 8 blocks appears once.
All inputs are finite; a program needn't handle non-finite values.
Results may differ from a plain program's by a relative error of at most 0.0095.
The roundings to bfloat16 on the way count: a program that leaves them out, or rounds other values in their place, can miss the bound.
Values may be sent and summed in bfloat16 or wider, within the bound.
No kernel may reach another device: no remote copies, remote signals or barrier semaphores. Data moves between devices by JAX's collectives and lax.ppermute only.
A program may use at most 64 MiB of HBM per device.

v0:
```python
import math
import jax
import jax.numpy as jnp
from jax import lax
from jax.sharding import PartitionSpec as P

HD = 128
GROUP = 4
BLOCK = 128
norm_epsilon = 1e-05
rotary_base = 500000.0
masked_score = -1e30


def passed_along(block, axis, distance):
    devices = range(lax.axis_size(axis))
    route = [((i - distance) % len(devices), i) for i in devices]
    return lax.ppermute(block, axis, route)


def session_starts(session_ids):
    length = session_ids.shape[0]
    indices = jnp.arange(length, dtype=jnp.int32)
    fresh = jnp.concatenate([jnp.ones((1,), dtype=jnp.bool_), session_ids[1:] != session_ids[:-1]])
    return lax.cummax(jnp.where(fresh, indices, 0), axis=0)


def rotary(vectors, position):
    half_dim = vectors.shape[-1] // 2
    ladder = jnp.arange(half_dim, dtype=jnp.float32) * (2.0 / vectors.shape[-1])
    frequency = jnp.exp(-ladder * math.log(rotary_base))
    angles = position.astype(jnp.float32).reshape((-1,) + (1,) * (vectors.ndim - 1)) * frequency
    cosine = jnp.cos(angles)
    sines = jnp.sin(angles)
    first_half = vectors[..., :half_dim]
    second_half = vectors[..., half_dim:]
    return jnp.concatenate(
        [first_half * cosine - second_half * sines, second_half * cosine + first_half * sines],
        axis=-1,
    )


def attend_core(
    carry_state, query_heads, query_pos, query_seg, key_heads, value_heads, key_pos, key_seg
):
    row_max, row_sum, mixed_sum = carry_state
    scores = jnp.einsum(
        "qagd,kad->qagk", query_heads, key_heads, preferred_element_type=jnp.float32
    ) * (1.0 / math.sqrt(query_heads.shape[-1]))
    allowed = ((query_seg[:, None] == key_seg[None, :]) & (key_pos[None, :] <= query_pos[:, None]))[
        :, None, None, :
    ]
    new_max = jnp.maximum(row_max, jnp.max(jnp.where(allowed, scores, masked_score), axis=-1))
    weights = jnp.where(allowed, jnp.exp(scores - new_max[..., None]), 0.0)
    rescale = jnp.exp(row_max - new_max)
    row_sum = row_sum * rescale + jnp.sum(weights, axis=-1)
    mixed_sum = mixed_sum * rescale[..., None] + jnp.einsum(
        "qagk,kad->qagd",
        weights.astype(jnp.bfloat16),
        value_heads,
        preferred_element_type=jnp.float32,
    )
    return (new_max, row_sum, mixed_sum)


def per_device(hidden_in, norm_gain, w_query, w_key, w_value, w_out, session_ids, block_anchor):
    whole, gain_full = (
        lax.all_gather(hidden_in, "head", axis=1, tiled=True),
        lax.all_gather(norm_gain, "head", axis=0, tiled=True),
    )
    tok_rows = whole.shape[0]
    cycle_size = lax.axis_size("ctx")
    cycle_index = lax.axis_index("ctx")
    per_shard = tok_rows // BLOCK
    starts = session_starts(session_ids)
    seg_table = session_ids.reshape(-1, BLOCK)
    start_table = starts.reshape(-1, BLOCK)
    offsets = jnp.arange(BLOCK, dtype=jnp.int32)

    def token_info(owner):
        blocks_here = lax.dynamic_slice_in_dim(block_anchor, owner * per_shard, per_shard)
        contiguous = (blocks_here[:, None] * BLOCK + offsets[None, :]).reshape(-1)
        session = jnp.take(seg_table, blocks_here, axis=0).reshape(-1)
        position = contiguous - jnp.take(start_table, blocks_here, axis=0).reshape(-1)
        return (contiguous, session, position)

    wide = whole.astype(jnp.float32)
    normed = (
        wide
        * lax.rsqrt(jnp.mean(wide * wide, axis=-1, keepdims=True) + norm_epsilon)
        * gain_full.astype(jnp.float32)
    ).astype(jnp.bfloat16)
    key_cols = w_key.shape[1]
    kv_local = key_cols // HD
    pieces = (
        lax.all_gather(w_query, "ctx", axis=0, tiled=True),
        lax.all_gather(w_key, "ctx", axis=0, tiled=True),
        lax.all_gather(w_value, "ctx", axis=0, tiled=True),
    )
    query_raw, key_raw, value_raw = tuple(
        (jnp.dot(normed, weight_rows, preferred_element_type=jnp.float32) for weight_rows in pieces)
    )
    my_pos, my_seg, my_place = token_info(cycle_index)
    query_heads = rotary(query_raw.reshape(tok_rows, kv_local, GROUP, HD), my_place).astype(
        jnp.bfloat16
    )
    key_heads = rotary(key_raw.reshape(tok_rows, kv_local, HD), my_place).astype(jnp.bfloat16)
    value_heads = value_raw.astype(jnp.bfloat16).reshape(tok_rows, kv_local, HD)

    def attend(current_state, kv_stack, source):
        key_pos, key_seg, unused_place = token_info(source)
        return attend_core(
            current_state, query_heads, my_pos, my_seg, kv_stack[0], kv_stack[1], key_pos, key_seg
        )

    carry_state = (
        jnp.full((tok_rows, kv_local, GROUP), masked_score, jnp.float32),
        jnp.zeros((tok_rows, kv_local, GROUP), jnp.float32),
        jnp.zeros((tok_rows, kv_local, GROUP, HD), jnp.float32),
    )
    own_stack = jnp.stack([key_heads, value_heads])
    carry_state = attend(carry_state, own_stack, cycle_index)

    def cycle_turn(turn_index, loop_carry):
        current_state, moving = loop_carry
        moving = passed_along(moving, "ctx", 1)
        current_state = attend(current_state, moving, (cycle_index - turn_index) % cycle_size)
        return (current_state, moving)

    carry_state, unused_stack = lax.fori_loop(1, cycle_size, cycle_turn, (carry_state, own_stack))
    final_max, row_sum, mixed_sum = carry_state
    attended = (mixed_sum / row_sum[..., None]).astype(jnp.bfloat16).reshape(tok_rows, -1)
    terms = jnp.dot(
        attended,
        lax.all_gather(w_out, "ctx", axis=1, tiled=True),
        preferred_element_type=jnp.float32,
    )
    return lax.psum_scatter(terms.astype(jnp.bfloat16), "head", scatter_dimension=1, tiled=True)


def solution(mesh):
    in_specs = (
        P(("groups", "ctx"), "head"),
        P("head"),
        P("ctx", "head"),
        P("ctx", "head"),
        P("ctx", "head"),
        P("head", "ctx"),
        P("groups"),
        P("groups"),
    )
    out_specs = P(("groups", "ctx"), "head")
    return jax.shard_map(
        per_device, mesh=mesh, in_specs=in_specs, out_specs=out_specs, check_vma=False
    )
```

profile of v0, /device:TPU:0, one launch (start us, length us, event | category | flops | bytes accessed | tf_op | source)
XLA Modules:
  0.0 302.0 jit_solution(423023249203372490)
XLA Ops:
  6.5 0.7 all-gather.6.cloned.1.call-update
  7.3 0.7 all-gather.8.cloned.1.call-update
  8.1 0.7 all-gather.12.cloned.1.call-update
  10.0 0.7 broadcast_multiply_fusion.1
  10.7 0.7 compare_and_fusion.3
  11.4 0.8 slice_compare_fusion
  12.3 1.2 gather_fusion.1
  13.7 6.3 %all_gather.19 = bf16[4096]{0:T(1024)(128)(2,1)S(1)} all-gather(bf16[1024]{0:T(1024)(128)(2,1)} %param.13), channel_id=1, replica_groups=mesh['groups'=2,'ctx'=4,'head'=4] {'head'}, dimensions={0}, use_global_device_ids=true | all-gather | bytes 10240 | tf_op jit(solution)/shard_map/all_gather | solution.py:69
  20.7 0.6 gather_fusion.2
  22.0 12.2 %all-gather.6.cloned.1.call-done = bf16[256,4096]{1,0:T(8,128)(2,1)} async-done(((bf16[256,1024]{1,0:T(8,128)(2,1)}), bf16[256,4096]{1,0:T(8,128)(2,1)}) %all-gather.6.cloned.1.call-update) | async-done | bytes 2097168 | tf_op jit(solution)/shard_map/all_gather | solution.py:68
  34.2 2.2 fusion.17
  36.5 27.3 %all-gather.8.cloned.1.call-done = bf16[4096,128]{1,0:T(8,128)(2,1)} async-done(((bf16[1024,128]{1,0:T(8,128)(2,1)}), bf16[4096,128]{1,0:T(8,128)(2,1)}) %all-gather.8.cloned.1.call-update) | async-done | bytes 1048592 | tf_op jit(solution)/shard_map/all_gather | solution.py:97
  63.8 2.8 convolution_bitcast_fusion.2
  66.9 25.8 %all-gather.12.cloned.1.call-done = bf16[4096,128]{1,0:T(8,128)(2,1)} async-done(((bf16[1024,128]{1,0:T(8,128)(2,1)}), bf16[4096,128]{1,0:T(8,128)(2,1)}) %all-gather.12.cloned.1.call-update) | async-done | bytes 1048592 | tf_op jit(solution)/shard_map/all_gather | solution.py:98
  92.8 2.2 convolution_convert_fusion.1
  95.1 79.2 %all-gather.10.cloned.1.call-done = bf16[4096,512]{1,0:T(8,128)(2,1)} async-done(((bf16[1024,512]{1,0:T(8,128)(2,1)}), bf16[4096,512]{1,0:T(8,128)(2,1)}) %all-gather.10.cloned.1.call-update) | async-done | bytes 4194320 | tf_op jit(solution)/shard_map/all_gather | solution.py:96
  174.4 3.5 %fusion.49 = f32[256,512]{1,0:T(8,128)S(1)} fusion(bf16[4096,512]{1,0:T(8,128)(2,1)} %all-gather.10.cloned.1.call-done, bf16[256,4096]{1,0:T(8,128)(2,1)S(1)} %copy-done, f32[4096]{0:T(1024)S(1)} %convert_element_type.65, f32[256]{0:T(256)S(1)} %add_rsqrt_fusion), kind=kOutput, calls=%fused_computation.101 | convolution fusion | flops 1077936128 | bytes 6833152 | tf_op jit(solution)/shard_map/dot_general | solution.py:101
  179.9 30.9 %while.22 = (s32[]{:T(128)}, f32[256,1,4]{0,2,1:T(4,128)S(1)}, f32[256,1,4]{0,2,1:T(4,128)S(1)}, f32[256,1,4,128]{3,0,2,1:T(8,128)S(1)}, bf16[2,256,1,128]{3,1,2...) while((s32[]{:T(128)}, f32[256,1,4]{0,2,1:T(4,128)S(1)}, ...), condition=%wide.region_8.10_spmd.clone, body=%wide.region_5.9_spmd.clone.sunk | while | flops 137040672 | bytes 5716408 | solution.py:130
  181.1 6.0 %collective-permute-done = bf16[2,256,1,128]{3,1,2,0:T(8,128)(2,1)S(1)} collective-permute-done((bf16[2,256,1,128]{3,1,2,0:T(8,128)(2,1)S(1)}, bf16[2,256,1,128]{3,1,2,0:T(8,128)(2,1)S(1)}, u32[]{:S(2)}, u32[]{:S(2)}) %collective-permute-start) | collective-permute-done | bytes 131104 | tf_op jit(solution)/shard_map/while/body/eval_jaxpr/ppermute | solution.py:18
  189.2 9.2 %collective-permute-done = bf16[2,256,1,128]{3,1,2,0:T(8,128)(2,1)S(1)} collective-permute-done((bf16[2,256,1,128]{3,1,2,0:T(8,128)(2,1)S(1)}, bf16[2,256,1,128]{3,1,2,0:T(8,128)(2,1)S(1)}, u32[]{:S(2)}, u32[]{:S(2)}) %collective-permute-start) | collective-permute-done | bytes 131104 | tf_op jit(solution)/shard_map/while/body/eval_jaxpr/ppermute | solution.py:18
  200.7 9.0 %collective-permute-done = bf16[2,256,1,128]{3,1,2,0:T(8,128)(2,1)S(1)} collective-permute-done((bf16[2,256,1,128]{3,1,2,0:T(8,128)(2,1)S(1)}, bf16[2,256,1,128]{3,1,2,0:T(8,128)(2,1)S(1)}, u32[]{:S(2)}, u32[]{:S(2)}) %collective-permute-start) | collective-permute-done | bytes 131104 | tf_op jit(solution)/shard_map/while/body/eval_jaxpr/ppermute | solution.py:18
  211.1 49.6 %all-gather.14.cloned.1.call-done = bf16[512,4096]{1,0:T(8,128)(2,1)} async-done(((bf16[512,1024]{1,0:T(8,128)(2,1)}), bf16[512,4096]{1,0:T(8,128)(2,1)}) %all-gather.14.cloned.1.call-update) | async-done | bytes 4194320 | tf_op jit(solution)/shard_map/all_gather | solution.py:135
  260.7 4.8 %convolution_convert_fusion = bf16[256,4096]{1,0:T(8,128)(2,1)} fusion(bf16[256,512]{0,1:T(8,128)(2,1)S(1)} %bitcast.132, bf16[512,4096]{1,0:T(8,128)(2,1)} %all-gather.14.cloned.1.call-done), kind=kOutput, calls=%fused_computation.36 | convolution fusion | flops 1074790400 | bytes 6553600 | tf_op jit(solution)/shard_map/dot_general | solution.py:133
  265.5 29.7 %reduce-scatter.2.cloned.1.call-done = bf16[256,1024]{1,0:T(8,128)(2,1)} async-done(((bf16[256,4096]{1,0:T(8,128)(2,1)}), bf16[256,1024]{1,0:T(8,128)(2,1)}) %reduce-scatter.2.cloned.1.call-update) | async-done | bytes 524304 | tf_op jit(solution)/shard_map/reduce_scatter | solution.py:138
  (91 shorter events, 12.1 us)
Async XLA Ops:
  6.5 27.7 %all-gather.6.cloned.1.call-start = ((), (), s32[]{:S(2)}) async-start(), calls=%async_computation.1 | async-start | bytes 2621440 | tf_op jit(solution)/shard_map/all_gather | solution.py:68
  7.3 56.5 %all-gather.8.cloned.1.call-start = ((), (), s32[]{:S(2)}) async-start(), calls=%async_computation.2 | async-start | bytes 1310720 | tf_op jit(solution)/shard_map/all_gather | solution.py:97
  8.0 84.8 %all-gather.12.cloned.1.call-start = ((), (), s32[]{:S(2)}) async-start(), calls=%async_computation.4 | async-start | bytes 1310720 | tf_op jit(solution)/shard_map/all_gather | solution.py:98
  8.7 165.6 %all-gather.10.cloned.1.call-start = ((), (), s32[]{:S(2)}) async-start(), calls=%async_computation.3 | async-start | bytes 5242880 | tf_op jit(solution)/shard_map/all_gather | solution.py:96
  9.3 251.4 %all-gather.14.cloned.1.call-start = ((), (), s32[]{:S(2)}) async-start(), calls=%async_computation.5 | async-start | bytes 5242880 | tf_op jit(solution)/shard_map/all_gather | solution.py:135
  9.9 285.3 %reduce-scatter.2.cloned.1.call-start = ((), (), s32[]{:S(2)}) async-start(), calls=%async_computation.6 | async-start | bytes 2621440 | tf_op jit(solution)/shard_map/reduce_scatter | solution.py:138
  34.2 58.6 %copy-start = (bf16[256,4096]{1,0:T(8,128)(2,1)S(1)}, bf16[256,4096]{1,0:T(8,128)(2,1)}, u32[]{:S(2)}) copy-start(bf16[256,4096]{1,0:T(8,128)(2,1)} %all-gather.6.cloned.1.call-done) | copy-start | bytes 6291460
  178.4 1.6 copy-start.1
  178.4 1.6 copy-start.2
  179.9 7.1 %collective-permute-start = (bf16[2,256,1,128]{3,1,2,0:T(8,128)(2,1)S(1)}, bf16[2,256,1,128]{3,1,2,0:T(8,128)(2,1)S(1)}, u32[]{:S(2)}, u32[]{:S(2)}) collective-permute-start(bf16[2,256,1,128]{3,1,2,0:T(8,128)(2,1)S(1)} %get-tuple-element.504), channel_id=1, source_target_pairs={{12,0},{0,4},{4,8},{8,12},{13,1},{1,5},{5,9},{9,13},{14,2},{2,6},{... | collective-permute-start | bytes 393224 | tf_op jit(solution)/shard_map/while/body/eval_jaxpr/ppermute | solution.py:18
  188.1 10.3 %collective-permute-start = (bf16[2,256,1,128]{3,1,2,0:T(8,128)(2,1)S(1)}, bf16[2,256,1,128]{3,1,2,0:T(8,128)(2,1)S(1)}, u32[]{:S(2)}, u32[]{:S(2)}) collective-permute-start(bf16[2,256,1,128]{3,1,2,0:T(8,128)(2,1)S(1)} %get-tuple-element.504), channel_id=1, source_target_pairs={{12,0},{0,4},{4,8},{8,12},{13,1},{1,5},{5,9},{9,13},{14,2},{2,6},{... | collective-permute-start | bytes 393224 | tf_op jit(solution)/shard_map/while/body/eval_jaxpr/ppermute | solution.py:18
  199.6 10.1 %collective-permute-start = (bf16[2,256,1,128]{3,1,2,0:T(8,128)(2,1)S(1)}, bf16[2,256,1,128]{3,1,2,0:T(8,128)(2,1)S(1)}, u32[]{:S(2)}, u32[]{:S(2)}) collective-permute-start(bf16[2,256,1,128]{3,1,2,0:T(8,128)(2,1)S(1)} %get-tuple-element.504), channel_id=1, source_target_pairs={{12,0},{0,4},{4,8},{8,12},{13,1},{1,5},{5,9},{9,13},{14,2},{2,6},{... | collective-permute-start | bytes 393224 | tf_op jit(solution)/shard_map/while/body/eval_jaxpr/ppermute | solution.py:18
Sparse Core Ops, SparseCore 0:
  8.9 25.2 all-gather.5
  35.8 27.9 all-gather.7
  65.4 27.3 all-gather.11
  94.2 80.1 all-gather.9
  175.8 84.8 all-gather.13
  265.6 29.4 reduce-scatter.1
where the time goes:
time: 302 us
  waiting for transfers between devices  251 us (83%)
  matrix products  16.6 us (5%)
  between operations  13.6 us (5%)
  other arithmetic  8.92 us (3%)
  blocking collectives  6.32 us (2%)
  local copies, waits for them, and re-layouts  4.74 us (2%)
    all_gather x1, waiting for transfers between devices, per_device(): lax.all_gather(w_query, 'ctx', axis=0, tiled=True)  79.2 us
    all_gather x1, waiting for transfers between devices, per_device(): lax.all_gather(w_out, 'ctx', axis=1, tiled=True)  49.6 us
    reduce_scatter x1, waiting for transfers between devices, per_device(): lax.psum_scatter(terms.astype(jnp.bfloat16), 'head', scatter_dimension=1,...  29.7 us
    all_gather x1, waiting for transfers between devices, per_device(): lax.all_gather(w_key, 'ctx', axis=0, tiled=True)  27.3 us
    all_gather x1, waiting for transfers between devices, per_device(): lax.all_gather(w_value, 'ctx', axis=0, tiled=True)  25.8 us
    ppermute x3, waiting for transfers between devices, passed_along(): return lax.ppermute(block, axis, route)  24.2 us
    all_gather x1, waiting for transfers between devices, per_device(): lax.all_gather(hidden_in, 'head', axis=1, tiled=True)  12.2 us
    dot_general x3, matrix products, per_device(): jnp.dot(normed, weight_rows, preferred_element_type=jnp.float32)  8.49 us
  transfers between devices with their start and end apart: 9, of which 9 were waited for; matrix products, arithmetic and copies ran while one was open for 8% of the time, Pallas kernels for 0%

commit v1 on v0

--- a/solution.py
+++ b/solution.py
@@ -93,7 +93,9 @@
     key_cols = w_key.shape[1]
     kv_local = key_cols // HD
     pieces = (
-        lax.all_gather(w_query, "ctx", axis=0, tiled=True),
+        jnp.concatenate(
+            lax.all_to_all(jnp.stack([w_query] * lax.axis_size("ctx")), "ctx", 0, 0), axis=0
+        ),
         lax.all_gather(w_key, "ctx", axis=0, tiled=True),
         lax.all_gather(w_value, "ctx", axis=0, tiled=True),
     )

time: 302 us -> 277 us (0.917)
  waiting for transfers between devices: 251 us -> 207 us
  local copies, waits for them, and re-layouts: 4.74 us -> 20.7 us
  starting transfers between devices: 0.37 us -> 6.77 us
    all_gather x1 -> x0, waiting for transfers between devices: 79.2 us -> none  [per_device(): lax.all_gather(w_query, 'ctx', axis=0, tiled=True)]
    all_gather x1, waiting for transfers between devices: 25.8 us -> 63.9 us  [per_device(): lax.all_gather(w_value, 'ctx', axis=0, tiled=True)]
    all_gather x1, waiting for transfers between devices: 49.6 us -> 31.4 us  [per_device(): lax.all_gather(w_out, 'ctx', axis=1, tiled=True)]
    all_gather x1, waiting for transfers between devices: 27.3 us -> 42.4 us  [per_device(): lax.all_gather(w_key, 'ctx', axis=0, tiled=True)]
    ppermute x3, waiting for transfers between devices: 24.2 us -> 31 us  [passed_along(): return lax.ppermute(block, axis, route)]
    dot_general x0 -> x1, local copies, waits for them, and re-layouts: none -> 6.59 us  [per_device(): jnp.dot(normed, weight_rows, preferred_element_type=jnp.float32)]
    all_to_all x0 -> x1, starting transfers between devices: none -> 6.48 us  [per_device(): lax.all_to_all(jnp.stack([w_query] * lax.axis_size('ctx')), 'ctx', 0, 0)]
    all_to_all x0 -> x1, local copies, waits for them, and re-layouts: none -> 6.35 us  [per_device(): lax.all_to_all(jnp.stack([w_query] * lax.axis_size('ctx')), 'ctx', 0, 0)]
  transfers between devices with their start and end apart: 9 -> 9, of which waited for: 9 -> 8; matrix products, arithmetic and copies ran while one was open for 8% -> 14% of each run, Pallas kernels for 0% -> 0%
where the time goes in v1:
time: 277 us
  waiting for transfers between devices  207 us (75%)
  local copies, waits for them, and re-layouts  20.7 us (7%)
  matrix products  16.5 us (6%)
  between operations  13.3 us (5%)
  starting transfers between devices  6.77 us (2%)
  other arithmetic  6.44 us (2%)
  blocking collectives  5.36 us (2%)
    all_gather x1, waiting for transfers between devices, per_device(): lax.all_gather(w_value, 'ctx', axis=0, tiled=True)  63.9 us
    all_gather x1, waiting for transfers between devices, per_device(): lax.all_gather(w_key, 'ctx', axis=0, tiled=True)  42.4 us
    all_gather x1, waiting for transfers between devices, per_device(): lax.all_gather(w_out, 'ctx', axis=1, tiled=True)  31.4 us
    ppermute x3, waiting for transfers between devices, passed_along(): return lax.ppermute(block, axis, route)  31 us
    reduce_scatter x1, waiting for transfers between devices, per_device(): lax.psum_scatter(terms.astype(jnp.bfloat16), 'head', scatter_dimension=1,...  29.8 us
    dot_general x3, matrix products, per_device(): jnp.dot(normed, weight_rows, preferred_element_type=jnp.float32)  8.59 us
    dot_general x1, local copies, waits for them, and re-layouts, per_device(): jnp.dot(normed, weight_rows, preferred_element_type=jnp.float32)  6.59 us
    all_to_all x1, starting transfers between devices, per_device(): lax.all_to_all(jnp.stack([w_query] * lax.axis_size('ctx')), 'ctx', 0, 0)  6.48 us
  transfers between devices with their start and end apart: 9, of which 8 were waited for; matrix products, arithmetic and copies ran while one was open for 14% of the time, Pallas kernels for 0%

profile of v1, /device:TPU:0, one launch (start us, length us, event | category | flops | bytes accessed | tf_op | source)
XLA Modules:
  0.0 276.7 jit_solution(15276924408257461483)
XLA Ops:
  6.5 0.7 all-gather.5.cloned.1.call-update
  7.3 0.7 all-gather.7.cloned.1.call-update
  8.0 1.5 copy.39
  9.5 2.5 stack.4
  12.0 6.5 %all-to-all-start = ((bf16[4,1024,512]{1,2,0:T(8,128)(2,1)}), bf16[4,1024,512]{1,2,0:T(8,128)(2,1)}, u32[]{:S(2)}, u32[]{:S(2)}) async-start(bf16[4,1024,512]{1,2,0:T(8,128)(2,1)} %stack.4), calls=%async_computation | async-start | bytes 8388608 | tf_op jit(solution)/shard_map/all_to_all | solution.py:97
  18.5 0.7 all-gather.9.cloned.1.call-update
  19.9 5.4 %all_gather.16 = bf16[4096]{0:T(1024)(128)(2,1)S(1)} all-gather(bf16[1024]{0:T(1024)(128)(2,1)S(1)} %copy-done.3), channel_id=1, replica_groups=mesh['groups'=2,'ctx'=4,'head'=4] {'head'}, dimensions={0}, use_global_device_ids=true | all-gather | bytes 10240 | tf_op jit(solution)/shard_map/all_gather | solution.py:69
  26.6 0.6 gather_fusion.2
  28.0 6.2 %all-gather.5.cloned.1.call-done = bf16[256,4096]{1,0:T(8,128)(2,1)} async-done(((bf16[256,1024]{1,0:T(8,128)(2,1)}), bf16[256,4096]{1,0:T(8,128)(2,1)}) %all-gather.5.cloned.1.call-update) | async-done | bytes 2097168 | tf_op jit(solution)/shard_map/all_gather | solution.py:68
  34.3 2.2 fusion.17
  36.5 42.4 %all-gather.7.cloned.1.call-done = bf16[4096,128]{1,0:T(8,128)(2,1)} async-done(((bf16[1024,128]{1,0:T(8,128)(2,1)}), bf16[4096,128]{1,0:T(8,128)(2,1)}) %all-gather.7.cloned.1.call-update) | async-done | bytes 1048592 | tf_op jit(solution)/shard_map/all_gather | solution.py:99
  78.9 2.8 %convolution_bitcast_fusion.2 = f32[256,1,128]{0,2,1:T(8,128)S(1)} fusion(bf16[4096,128]{1,0:T(8,128)(2,1)} %all-gather.7.cloned.1.call-done, bf16[256,4096]{1,0:T(8,128)(2,1)} %all-gather.5.cloned.1.call-done, f32[4096]{0:T(1024)S(1)} %convert_element_type.65, f32[256]{0:T(256)S(1)} %add_rsqrt_fusion), kind=kOutput, calls=%fused_computation.48 | convolution fusion | flops 272629760 | bytes 3294208 | tf_op jit(solution)/shard_map/dot_general | solution.py:103
  82.1 63.9 %all-gather.9.cloned.1.call-done = bf16[4096,128]{1,0:T(8,128)(2,1)} async-done(((bf16[1024,128]{1,0:T(8,128)(2,1)}), bf16[4096,128]{1,0:T(8,128)(2,1)}) %all-gather.9.cloned.1.call-update) | async-done | bytes 1048592 | tf_op jit(solution)/shard_map/all_gather | solution.py:100
  145.9 2.2 convolution_convert_fusion.1
  148.3 6.4 %copy.40 = bf16[4,1024,512]{2,1,0:T(8,128)(2,1)} copy(bf16[4,1024,512]{1,2,0:T(8,128)(2,1)} %all-to-all-done) | data formatting | bytes 8388608 | tf_op jit(solution)/shard_map/all_to_all | solution.py:97
  154.6 6.6 %copy.41 = bf16[512,4096]{1,0:T(8,128)(2,1)} copy(bf16[512,4096]{0,1:T(8,128)(2,1)} %bitcast.139) | data formatting | bytes 8388608 | tf_op jit(solution)/shard_map/dot_general | solution.py:103
  161.2 3.6 %fusion.23 = f32[256,1,4,128]{0,3,2,1:T(8,128)S(1)} fusion(bf16[4,128,4096]{2,1,0:T(8,128)(2,1)} %bitcast.140, bf16[256,4096]{1,0:T(8,128)(2,1)S(1)} %copy-done, f32[4096]{0:T(1024)S(1)} %convert_element_type.65, f32[256]{0:T(256)S(1)} %add_rsqrt_fusion), kind=kOutput, calls=%fused_computation.44 | convolution fusion | flops 1077936128 | bytes 6833152 | tf_op jit(solution)/shard_map/dot_general | solution.py:103
  166.2 37.6 %while.22 = (s32[]{:T(128)}, f32[256,1,4]{0,2,1:T(4,128)S(1)}, f32[256,1,4]{0,2,1:T(4,128)S(1)}, f32[256,1,4,128]{3,0,2,1:T(8,128)S(1)}, bf16[2,256,1,128]{3,1,2...) while((s32[]{:T(128)}, f32[256,1,4]{0,2,1:T(4,128)S(1)}, ...), condition=%wide.region_8.10_spmd.clone, body=%wide.region_5.9_spmd.clone.sunk | while | flops 137040672 | bytes 5716408 | solution.py:132
  167.4 9.6 %collective-permute-done = bf16[2,256,1,128]{3,1,2,0:T(8,128)(2,1)S(1)} collective-permute-done((bf16[2,256,1,128]{3,1,2,0:T(8,128)(2,1)S(1)}, bf16[2,256,1,128]{3,1,2,0:T(8,128)(2,1)S(1)}, u32[]{:S(2)}, u32[]{:S(2)}) %collective-permute-start) | collective-permute-done | bytes 131104 | tf_op jit(solution)/shard_map/while/body/eval_jaxpr/ppermute | solution.py:18
  179.2 9.5 %collective-permute-done = bf16[2,256,1,128]{3,1,2,0:T(8,128)(2,1)S(1)} collective-permute-done((bf16[2,256,1,128]{3,1,2,0:T(8,128)(2,1)S(1)}, bf16[2,256,1,128]{3,1,2,0:T(8,128)(2,1)S(1)}, u32[]{:S(2)}, u32[]{:S(2)}) %collective-permute-start) | collective-permute-done | bytes 131104 | tf_op jit(solution)/shard_map/while/body/eval_jaxpr/ppermute | solution.py:18
  190.9 11.9 %collective-permute-done = bf16[2,256,1,128]{3,1,2,0:T(8,128)(2,1)S(1)} collective-permute-done((bf16[2,256,1,128]{3,1,2,0:T(8,128)(2,1)S(1)}, bf16[2,256,1,128]{3,1,2,0:T(8,128)(2,1)S(1)}, u32[]{:S(2)}, u32[]{:S(2)}) %collective-permute-start) | collective-permute-done | bytes 131104 | tf_op jit(solution)/shard_map/while/body/eval_jaxpr/ppermute | solution.py:18
  204.2 31.4 %all-gather.11.cloned.1.call-done = bf16[512,4096]{1,0:T(8,128)(2,1)} async-done(((bf16[512,1024]{1,0:T(8,128)(2,1)}), bf16[512,4096]{1,0:T(8,128)(2,1)}) %all-gather.11.cloned.1.call-update) | async-done | bytes 4194320 | tf_op jit(solution)/shard_map/all_gather | solution.py:137
  235.6 4.8 %convolution_convert_fusion = bf16[256,4096]{1,0:T(8,128)(2,1)} fusion(bf16[256,512]{0,1:T(8,128)(2,1)S(1)} %bitcast.143, bf16[512,4096]{1,0:T(8,128)(2,1)} %all-gather.11.cloned.1.call-done), kind=kOutput, calls=%fused_computation.36 | convolution fusion | flops 1074790400 | bytes 6553600 | tf_op jit(solution)/shard_map/dot_general | solution.py:135
  240.4 29.8 %reduce-scatter.2.cloned.1.call-done = bf16[256,1024]{1,0:T(8,128)(2,1)} async-done(((bf16[256,4096]{1,0:T(8,128)(2,1)}), bf16[256,1024]{1,0:T(8,128)(2,1)}) %reduce-scatter.2.cloned.1.call-update) | async-done | bytes 524304 | tf_op jit(solution)/shard_map/reduce_scatter | solution.py:140
  (95 shorter events, 11.4 us)
Async XLA Ops:
  6.5 27.7 %all-gather.5.cloned.1.call-start = ((), (), s32[]{:S(2)}) async-start(), calls=%async_computation.2 | async-start | bytes 2621440 | tf_op jit(solution)/shard_map/all_gather | solution.py:68
  7.3 71.7 %all-gather.7.cloned.1.call-start = ((), (), s32[]{:S(2)}) async-start(), calls=%async_computation.3 | async-start | bytes 1310720 | tf_op jit(solution)/shard_map/all_gather | solution.py:99
  12.0 7.8 %copy-start.3 = (bf16[1024]{0:T(1024)(128)(2,1)S(1)}, bf16[1024]{0:T(1024)(128)(2,1)}, u32[]{:S(2)}) copy-start(bf16[1024]{0:T(1024)(128)(2,1)} %param.13) | copy-start | bytes 6148
  12.0 13.2 %copy-start.1 = (s32[1024]{0:T(1024)S(1)}, s32[1024]{0:T(1024)}, u32[]{:S(2)}) copy-start(s32[1024]{0:T(1024)} %param.18) | copy-start | bytes 12292
  12.0 13.8 %copy-start.2 = (s32[8]{0:T(128)S(1)}, s32[8]{0:T(128)}, u32[]{:S(2)}) copy-start(s32[8]{0:T(128)} %param.19) | copy-start | bytes 100
  12.0 136.3 %all-to-all-start = ((bf16[4,1024,512]{1,2,0:T(8,128)(2,1)}), bf16[4,1024,512]{1,2,0:T(8,128)(2,1)}, u32[]{:S(2)}, u32[]{:S(2)}) async-start(bf16[4,1024,512]{1,2,0:T(8,128)(2,1)} %stack.4), calls=%async_computation | async-start | bytes 8388608 | tf_op jit(solution)/shard_map/all_to_all | solution.py:97
  18.5 127.4 %all-gather.9.cloned.1.call-start = ((), (), s32[]{:S(2)}) async-start(), calls=%async_computation.4 | async-start | bytes 1310720 | tf_op jit(solution)/shard_map/all_gather | solution.py:100
  19.2 216.3 %all-gather.11.cloned.1.call-start = ((), (), s32[]{:S(2)}) async-start(), calls=%async_computation.5 | async-start | bytes 5242880 | tf_op jit(solution)/shard_map/all_gather | solution.py:137
  19.8 250.4 %reduce-scatter.2.cloned.1.call-start = ((), (), s32[]{:S(2)}) async-start(), calls=%async_computation.6 | async-start | bytes 2621440 | tf_op jit(solution)/shard_map/reduce_scatter | solution.py:140
  34.3 111.7 %copy-start = (bf16[256,4096]{1,0:T(8,128)(2,1)S(1)}, bf16[256,4096]{1,0:T(8,128)(2,1)}, u32[]{:S(2)}) copy-start(bf16[256,4096]{1,0:T(8,128)(2,1)} %all-gather.5.cloned.1.call-done) | copy-start | bytes 6291460
  166.3 10.7 %collective-permute-start = (bf16[2,256,1,128]{3,1,2,0:T(8,128)(2,1)S(1)}, bf16[2,256,1,128]{3,1,2,0:T(8,128)(2,1)S(1)}, u32[]{:S(2)}, u32[]{:S(2)}) collective-permute-start(bf16[2,256,1,128]{3,1,2,0:T(8,128)(2,1)S(1)} %get-tuple-element.513), channel_id=1, source_target_pairs={{12,0},{0,4},{4,8},{8,12},{13,1},{1,5},{5,9},{9,13},{14,2},{2,6},{... | collective-permute-start | bytes 393224 | tf_op jit(solution)/shard_map/while/body/eval_jaxpr/ppermute | solution.py:18
  178.1 10.6 %collective-permute-start = (bf16[2,256,1,128]{3,1,2,0:T(8,128)(2,1)S(1)}, bf16[2,256,1,128]{3,1,2,0:T(8,128)(2,1)S(1)}, u32[]{:S(2)}, u32[]{:S(2)}) collective-permute-start(bf16[2,256,1,128]{3,1,2,0:T(8,128)(2,1)S(1)} %get-tuple-element.513), channel_id=1, source_target_pairs={{12,0},{0,4},{4,8},{8,12},{13,1},{1,5},{5,9},{9,13},{14,2},{2,6},{... | collective-permute-start | bytes 393224 | tf_op jit(solution)/shard_map/while/body/eval_jaxpr/ppermute | solution.py:18
  189.8 13.0 %collective-permute-start = (bf16[2,256,1,128]{3,1,2,0:T(8,128)(2,1)S(1)}, bf16[2,256,1,128]{3,1,2,0:T(8,128)(2,1)S(1)}, u32[]{:S(2)}, u32[]{:S(2)}) collective-permute-start(bf16[2,256,1,128]{3,1,2,0:T(8,128)(2,1)S(1)} %get-tuple-element.513), channel_id=1, source_target_pairs={{12,0},{0,4},{4,8},{8,12},{13,1},{1,5},{5,9},{9,13},{14,2},{2,6},{... | collective-permute-start | bytes 393224 | tf_op jit(solution)/shard_map/while/body/eval_jaxpr/ppermute | solution.py:18
Sparse Core Ops, SparseCore 0:
  8.9 25.3 all-gather.4
  35.8 43.0 all-gather.6
  80.5 65.3 all-gather.8
  147.4 88.1 all-gather.10
  240.5 29.6 reduce-scatter.1
